TPU v7x, 256 devices: a whole 4x4x8 slice. The times are simulated.
256 devices in a mesh: rows: 16 (over x, y), sub: 16 (over z, core).
Axes of the slice: x: 4, y: 4, z: 8, core: 2. Of those that a mesh axis runs over, the one named last changes fastest.
Arguments:
- embeddings: bfloat16 [65536, 1024], P(('rows', 'sub'))
- codes: int32 [64, 65536], P(None, ('rows', 'sub')), may hold values from 0 to 255
- codebook: bfloat16 [256, 1024], P(None, 'sub'), may hold values from -6 to 6
Outputs:
- rotation: float32 [1024, 1024], P('sub')
- rotated: bfloat16 [65536, 1024], P(('rows', 'sub'))
- new_codebook: float32 [256, 1024], P(None, 'sub')
All inputs are finite; a program needn't handle non-finite values.
Results may differ from a plain program's by a relative error of at most 0.0095.
Values may be sent and summed in bfloat16 or wider, within the bound.
No kernel may reach another device: no remote copies, remote signals or barrier semaphores. Data moves between devices by JAX's collectives and lax.ppermute only.
A program may use at most 64 MiB of HBM per device.

v0:
```python
import math
import jax
import jax.numpy as jnp
from jax import lax
from jax.sharding import PartitionSpec as P

NS_STEPS = 3
coef_a = 3.4445
coef_b = -4.775
coef_c = 2.0315
frob_eps = 1e-07


def one_hot_codes(code_block, count_codes):
    levels = lax.broadcasted_iota(jnp.int32, code_block.shape + (count_codes,), 2)
    return (code_block[:, :, None] == levels).astype(jnp.bfloat16)


def decode_rows(codes, table):
    subspaces, local_rows = codes.shape
    count_codes, row_width = table.shape
    sub_width = row_width // subspaces
    codewords = table.reshape(count_codes, subspaces, sub_width)
    one_hot = one_hot_codes(codes, count_codes)
    picked = jnp.einsum("mnk,kmj->nmj", one_hot, codewords, preferred_element_type=jnp.float32)
    return picked.reshape(local_rows, row_width).astype(jnp.bfloat16)


def codeword_totals(codes, row_values, count_codes):
    subspaces, local_rows = codes.shape
    row_width = row_values.shape[1]
    sub_width = row_width // subspaces
    one_hot = one_hot_codes(codes, count_codes)
    pieces = row_values.reshape(local_rows, subspaces, sub_width)
    code_sums = jnp.einsum("mnk,nmj->kmj", one_hot, pieces, preferred_element_type=jnp.float32)
    counts = jnp.sum(one_hot, axis=1, dtype=jnp.float32).T
    return (code_sums.reshape(count_codes, row_width), counts)


def bdot(left, right, dims):
    return lax.dot_general(
        left.astype(jnp.bfloat16),
        right.astype(jnp.bfloat16),
        (dims, ((), ())),
        preferred_element_type=jnp.float32,
    )


def newton_step(z):
    z_half = z.astype(jnp.bfloat16)
    gram = bdot(z_half, z_half, ((1,), (1,)))
    quartic = bdot(gram, gram, ((1,), (0,)))
    mixer = coef_b * gram + coef_c * quartic
    return coef_a * z + bdot(mixer, z_half, ((1,), (0,)))


def body(embeddings, codes, codebook):
    table = lax.all_gather(codebook, "sub", axis=1, tiled=True)
    decoded = decode_rows(codes, table)
    partial = lax.dot_general(
        embeddings, decoded, (((0,), (0,)), ((), ())), preferred_element_type=jnp.float32
    )
    cross = lax.psum(partial, ("rows", "sub"))
    frob_scale = jnp.sqrt(jnp.sum(cross * cross)) + frob_eps
    z = cross / frob_scale
    for newton_step_index in range(NS_STEPS):
        z = newton_step(z)
    rotation_half = z.astype(jnp.bfloat16)
    rotated = jnp.dot(embeddings, rotation_half, preferred_element_type=jnp.float32).astype(
        jnp.bfloat16
    )
    code_sums, counts = codeword_totals(codes, rotated, table.shape[0])
    code_sums = lax.psum(code_sums, ("rows", "sub"))
    counts = lax.psum(counts, ("rows", "sub"))
    me = lax.axis_index("sub")
    cols = codebook.shape[1]
    own_subspaces = counts.shape[1] * cols // code_sums.shape[1]
    own_sums = lax.dynamic_slice_in_dim(code_sums, me * cols, cols, axis=1)
    own_counts = lax.dynamic_slice_in_dim(counts, me * own_subspaces, own_subspaces, axis=1)
    own_codebook = codebook.astype(jnp.float32)
    spread = jnp.repeat(own_counts, cols // own_subspaces, axis=1)
    new_codebook = (own_sums + own_codebook) / (spread + 1.0)
    panel_rows = z.shape[0] // lax.axis_size("sub")
    panel = lax.dynamic_slice_in_dim(z, me * panel_rows, panel_rows, axis=0)
    return (panel, rotated, new_codebook)


def solution(mesh):
    in_specs = (P(("rows", "sub"), None), P(None, ("rows", "sub")), P(None, "sub"))
    out_specs = (P("sub", None), P(("rows", "sub"), None), P(None, "sub"))
    return jax.shard_map(body, mesh=mesh, in_specs=in_specs, out_specs=out_specs, check_vma=False)
```

profile of v0, /device:TPU:6, one launch (start us, length us, event | category | flops | bytes accessed | tf_op | source)
XLA Modules:
  0.0 650.9 jit_solution(6691471587485620089)
XLA Ops:
  7.2 0.0 copy-start
  7.2 0.0 all-reduce.4.cloned.1.call-start
  7.2 21.8 %all_gather.3 = bf16[256,1024]{0,1:T(8,128)(2,1)S(1)} all-gather(bf16[256,64]{0,1:T(8,128)(2,1)} %param.5), channel_id=1, replica_groups=mesh['rows'=16,'sub'=16] {'sub'}, dimensions={1}, use_global_device_ids=true | all-gather | bytes 557056 | tf_op jit(solution)/shard_map/all_gather | solution.py:58
  29.0 5.3 fusion.14
  34.3 0.0 copy-done
  34.3 2.7 convolution_bitcast_fusion
  36.9 0.0 copy-start.2
  36.9 0.0 all-reduce.4.cloned.1.call-update
  37.0 0.0 all-reduce.6.cloned.1.call-start
  37.0 0.8 copy-done.2
  37.8 3.4 convert_reduce_fusion
  41.2 264.1 %all-reduce.4.cloned.1.call-done = f32[1024,1024]{0,1:T(8,128)} async-done(((f32[1024,1024]{0,1:T(8,128)}), f32[1024,1024]{0,1:T(8,128)}) %all-reduce.4.cloned.1.call-update) | async-done | bytes 4194320 | tf_op jit(solution)/shard_map/psum | solution.py:63
  305.3 3.9 multiply_reduce_fusion
  309.9 7.8 %fusion.28 = f32[1024,1024]{1,0:T(8,128)} fusion(f32[1024,1024]{0,1:T(8,128)} %all-reduce.4.cloned.1.call-done, f32[]{:T(128)S(6)} %add.47), kind=kOutput, calls=%fused_computation.30 | convolution fusion | flops 2149580800 | bytes 8388612 | tf_op jit(solution)/shard_map/dot_general | solution.py:41
  317.7 13.9 %multiply_add_fusion.2 = f32[1024,1024]{0,1:T(8,128)} fusion(f32[1024,1024]{0,1:T(8,128)} %all-reduce.4.cloned.1.call-done, f32[]{:T(128)S(6)} %add.47, f32[1024,1024]{1,0:T(8,128)} %fusion.28), kind=kOutput, calls=%fused_computation.12 | convolution fusion | flops 4305453056 | bytes 12582916 | tf_op jit(solution)/shard_map/dot_general | solution.py:41
  331.6 7.8 %fusion.21 = f32[1024,1024]{1,0:T(8,128)} fusion(f32[1024,1024]{0,1:T(8,128)} %multiply_add_fusion.2), kind=kOutput, calls=%fused_computation.28 | convolution fusion | flops 2148532224 | bytes 8388608 | tf_op jit(solution)/shard_map/dot_general | solution.py:41
  339.4 13.7 %multiply_add_fusion.1 = f32[1024,1024]{0,1:T(8,128)} fusion(f32[1024,1024]{0,1:T(8,128)} %multiply_add_fusion.2, f32[1024,1024]{1,0:T(8,128)} %fusion.21), kind=kOutput, calls=%fused_computation.10 | convolution fusion | flops 4303355904 | bytes 12582912 | tf_op jit(solution)/shard_map/dot_general | solution.py:41
  353.1 8.0 %fusion.18 = f32[1024,1024]{1,0:T(8,128)} fusion(f32[1024,1024]{0,1:T(8,128)} %multiply_add_fusion.1), kind=kOutput, calls=%fused_computation.25 | convolution fusion | flops 2148532224 | bytes 8388608 | tf_op jit(solution)/shard_map/dot_general | solution.py:41
  361.2 13.9 %multiply_add_fusion = f32[1024,1024]{0,1:T(8,128)} fusion(f32[1024,1024]{0,1:T(8,128)} %multiply_add_fusion.1, f32[1024,1024]{1,0:T(8,128)} %fusion.18), kind=kOutput, calls=%fused_computation.8 | convolution fusion | flops 4303355904 | bytes 12582912 | tf_op jit(solution)/shard_map/dot_general | solution.py:41
  375.1 2.9 fusion.11
  378.0 0.0 copy-start.1
  378.0 5.1 fusion.1
  383.1 0.0 all-reduce.6.cloned.1.call-update
  383.1 1.2 constant_dynamic-slice_fusion
  384.4 0.9 copy.9
  385.3 1.0 copy.10
  386.3 255.6 %all-reduce.6.cloned.1.call-done = (f32[256,1024]{0,1:T(8,128)}, f32[256,64]{0,1:T(8,128)}) async-done(((f32[256,1024]{0,1:T(8,128)}, f32[256,64]{0,1:T(8,128)}), (f32[256,1024]{0,1:T(8,128)}, f32[256,64]{0,1:T(8,128)})) %all-reduce.6.cloned.1.call-update) | async-done | bytes 1114128 | tf_op jit(solution)/shard_map/psum | solution.py:73
  641.9 0.7 dynamic-slice_add_fusion
  642.6 0.0 copy-done.1
  642.6 1.5 bitcast_divide_fusion
Async XLA Ops:
  7.2 27.1 %copy-start = (bf16[256,1024]{1,0:T(8,128)(2,1)S(1)}, bf16[256,1024]{1,0:T(8,128)(2,1)}, u32[]{:S(2)}) copy-start(bf16[256,1024]{1,0:T(8,128)(2,1)} %param.3) | copy-start | bytes 1572868
  7.2 298.1 %all-reduce.4.cloned.1.call-start = ((), (), s32[]{:S(2)}) async-start(), calls=%async_computation | async-start | bytes 8388608 | tf_op jit(solution)/shard_map/psum | solution.py:63
  36.9 0.8 copy-start.2
  37.0 604.9 %all-reduce.6.cloned.1.call-start = ((), (), s32[]{:S(2)}) async-start(), calls=%async_computation.1 | async-start | bytes 2228224 | tf_op jit(solution)/shard_map/psum | solution.py:73
  378.0 264.6 %copy-start.1 = (bf16[256,64]{0,1:T(8,128)(2,1)S(1)}, bf16[256,64]{0,1:T(8,128)(2,1)}, u32[]{:S(2)}) copy-start(bf16[256,64]{0,1:T(8,128)(2,1)} %param.5) | copy-start | bytes 98308
Sparse Core Ops, SparseCore 0:
  37.1 268.1 all-reduce.3
  383.3 258.5 all-reduce.5
where the time goes:
time: 652 us; the launch traced here: 651 us
  waiting for transfers between devices  520 us (80%)
  matrix products  81.1 us (12%)
  blocking collectives  21.8 us (3%)
  between operations  14.8 us (2%)
  other arithmetic  9.48 us (1%)
    psum x1, waiting for transfers between devices, body(): cross = lax.psum(partial, ('rows', 'sub'))  264 us
    psum x1, waiting for transfers between devices, body(): code_sums = lax.psum(code_sums, ('rows', 'sub'))  256 us
    dot_general x6, matrix products, bdot(): lax.dot_general(left.astype(jnp.bfloat16), right.astype(jnp.bfloat16), (d...  65.2 us
    all_gather x1, blocking collectives, body(): table = lax.all_gather(codebook, 'sub', axis=1, tiled=True)  21.8 us
  transfers between devices with their start and end apart: 2, of which 2 were waited for; matrix products, arithmetic and copies ran while one was open for 1% of the time, Pallas kernels for 0%

commit v1 on v0

--- a/solution.py
+++ b/solution.py
@@ -55,7 +55,23 @@
 
 
 def body(embeddings, codes, codebook):
-    table = lax.all_gather(codebook, "sub", axis=1, tiled=True)
+    size, here, rows = (lax.axis_size("sub"), lax.axis_index("sub"), codebook.shape[1])
+    forward = [(i, (i + 1) % size) for i in range(size)]
+    backward = [(i, (i - 1) % size) for i in range(size)]
+    table = jnp.zeros((*codebook.shape[:1], size * rows, *codebook.shape[1 + 1 :]), codebook.dtype)
+    table = lax.dynamic_update_slice_in_dim(table, codebook, here * rows, axis=1)
+    from_left = from_right = codebook
+    half = size // 2
+    for step in range(1, half + 1):
+        from_left = lax.ppermute(from_left, "sub", forward)
+        table = lax.dynamic_update_slice_in_dim(
+            table, from_left, (here - step) % size * rows, axis=1
+        )
+        if step < size - half:
+            from_right = lax.ppermute(from_right, "sub", backward)
+            table = lax.dynamic_update_slice_in_dim(
+                table, from_right, (here + step) % size * rows, axis=1
+            )
     decoded = decode_rows(codes, table)
     partial = lax.dot_general(
         embeddings, decoded, (((0,), (0,)), ((), ())), preferred_element_type=jnp.float32

time: 652 us -> 671 us (1.029)
  starting transfers between devices: 0.08 us -> 23 us
  blocking collectives: 21.8 us -> 0 us
  waiting for transfers between devices: 520 us -> 537 us
    ppermute x0 -> x15, starting transfers between devices: none -> 23 us  [the longest x7 22.9 us: body(): from_right = lax.ppermute(from_right, 'sub', backward)]
    all_gather x1 -> x0, blocking collectives: 21.8 us -> none  [body(): table = lax.all_gather(codebook, 'sub', axis=1, tiled=True)]
    ppermute x0 -> x15, waiting for transfers between devices: none -> 15.1 us  [the longest x8 14.8 us: body(): from_left = lax.ppermute(from_left, 'sub', forward)]
  transfers between devices with their start and end apart: 2 -> 17, of which waited for: 2 -> 11; matrix products, arithmetic and copies ran while one was open for 1% -> 1% of each run, Pallas kernels for 0% -> 0%
where the time goes in v1:
time: 671 us; the launch traced here: 670 us
  waiting for transfers between devices  537 us (80%)
  matrix products  81.1 us (12%)
  starting transfers between devices  23 us (3%)
  between operations  14.8 us (2%)
  other arithmetic  9.48 us (1%)
    psum x1, waiting for transfers between devices, body(): cross = lax.psum(partial, ('rows', 'sub'))  267 us
    psum x1, waiting for transfers between devices, body(): code_sums = lax.psum(code_sums, ('rows', 'sub'))  255 us
    dot_general x6, matrix products, bdot(): lax.dot_general(left.astype(jnp.bfloat16), right.astype(jnp.bfloat16), (d...  65.1 us
    ppermute x7, starting transfers between devices, body(): from_right = lax.ppermute(from_right, 'sub', backward)  22.9 us
    ppermute x8, waiting for transfers between devices, body(): from_left = lax.ppermute(from_left, 'sub', forward)  14.8 us
  transfers between devices with their start and end apart: 17, of which 11 were waited for; matrix products, arithmetic and copies ran while one was open for 1% of the time, Pallas kernels for 0%

profile of v1, /device:TPU:6, one launch (start us, length us, event | category | flops | bytes accessed | tf_op | source)
XLA Modules:
  0.0 670.4 jit_solution(8375686706223122576)
XLA Ops:
  7.2 0.0 all-reduce.4.cloned.1.call-start
  7.2 0.0 collective-permute-start
  7.3 5.3 collective-permute-start.1
  12.6 0.8 constant_dynamic-update-slice_fusion.15
  13.4 1.0 collective-permute-done
  14.3 0.1 collective-permute-done.1
  14.5 2.8 collective-permute-start.3
  17.3 1.6 collective-permute-done.2
  18.9 0.0 collective-permute-done.3
  18.9 3.0 collective-permute-start.5
  21.9 1.6 collective-permute-done.4
  23.5 0.0 collective-permute-done.5
  23.5 3.0 collective-permute-start.7
  26.4 1.6 collective-permute-done.6
  28.0 0.0 collective-permute-done.7
  28.0 3.0 collective-permute-start.9
  31.0 1.6 collective-permute-done.8
  32.6 0.0 collective-permute-done.9
  32.6 3.0 collective-permute-start.11
  35.5 1.6 collective-permute-done.10
  37.1 0.0 collective-permute-done.11
  37.1 3.0 collective-permute-start.13
  40.1 1.6 collective-permute-done.12
  41.7 0.0 collective-permute-done.13
  41.7 4.5 collective-permute-done.14
  46.2 5.3 fusion.14
  51.5 2.7 convolution_bitcast_fusion
  54.2 0.0 all-reduce.4.cloned.1.call-update
  54.2 0.0 all-reduce.6.cloned.1.call-start
  54.2 0.8 copy-done.2
  55.0 3.4 convert_reduce_fusion
  58.4 266.6 %all-reduce.4.cloned.1.call-done = f32[1024,1024]{0,1:T(8,128)} async-done(((f32[1024,1024]{0,1:T(8,128)}), f32[1024,1024]{0,1:T(8,128)}) %all-reduce.4.cloned.1.call-update) | async-done | bytes 4194320 | tf_op jit(solution)/shard_map/psum | solution.py:79
  325.0 3.9 multiply_reduce_fusion
  329.6 7.8 %fusion.28 = f32[1024,1024]{1,0:T(8,128)} fusion(f32[1024,1024]{0,1:T(8,128)} %all-reduce.4.cloned.1.call-done, f32[]{:T(128)S(6)} %add.206), kind=kOutput, calls=%fused_computation.30 | convolution fusion | flops 2149580800 | bytes 8388612 | tf_op jit(solution)/shard_map/dot_general | solution.py:41
  337.4 13.9 %multiply_add_fusion.2 = f32[1024,1024]{0,1:T(8,128)} fusion(f32[1024,1024]{0,1:T(8,128)} %all-reduce.4.cloned.1.call-done, f32[]{:T(128)S(6)} %add.206, f32[1024,1024]{1,0:T(8,128)} %fusion.28), kind=kOutput, calls=%fused_computation.12 | convolution fusion | flops 4305453056 | bytes 12582916 | tf_op jit(solution)/shard_map/dot_general | solution.py:41
  351.3 7.8 %fusion.21 = f32[1024,1024]{1,0:T(8,128)} fusion(f32[1024,1024]{0,1:T(8,128)} %multiply_add_fusion.2), kind=kOutput, calls=%fused_computation.28 | convolution fusion | flops 2148532224 | bytes 8388608 | tf_op jit(solution)/shard_map/dot_general | solution.py:41
  359.1 13.6 %multiply_add_fusion.1 = f32[1024,1024]{0,1:T(8,128)} fusion(f32[1024,1024]{0,1:T(8,128)} %multiply_add_fusion.2, f32[1024,1024]{1,0:T(8,128)} %fusion.21), kind=kOutput, calls=%fused_computation.10 | convolution fusion | flops 4303355904 | bytes 12582912 | tf_op jit(solution)/shard_map/dot_general | solution.py:41
  372.7 8.1 %fusion.18 = f32[1024,1024]{1,0:T(8,128)} fusion(f32[1024,1024]{0,1:T(8,128)} %multiply_add_fusion.1), kind=kOutput, calls=%fused_computation.25 | convolution fusion | flops 2148532224 | bytes 8388608 | tf_op jit(solution)/shard_map/dot_general | solution.py:41
  380.8 13.9 %multiply_add_fusion = f32[1024,1024]{0,1:T(8,128)} fusion(f32[1024,1024]{0,1:T(8,128)} %multiply_add_fusion.1, f32[1024,1024]{1,0:T(8,128)} %fusion.18), kind=kOutput, calls=%fused_computation.8 | convolution fusion | flops 4303355904 | bytes 12582912 | tf_op jit(solution)/shard_map/dot_general | solution.py:41
  394.7 2.9 fusion.11
  397.6 5.1 fusion.1
  402.8 0.0 all-reduce.6.cloned.1.call-update
  402.8 1.0 copy.10
  403.8 1.2 constant_dynamic-slice_fusion.1
  405.0 0.9 copy.9
  405.9 255.5 %all-reduce.6.cloned.1.call-done = (f32[256,1024]{0,1:T(8,128)}, f32[256,64]{0,1:T(8,128)}) async-done(((f32[256,1024]{0,1:T(8,128)}, f32[256,64]{0,1:T(8,128)}), (f32[256,1024]{0,1:T(8,128)}, f32[256,64]{0,1:T(8,128)})) %all-reduce.6.cloned.1.call-update) | async-done | bytes 1114128 | tf_op jit(solution)/shard_map/psum | solution.py:89
  661.4 0.7 fusion.30
  662.1 1.5 bitcast_divide_fusion
  (28 shorter events, 0.1 us)
Async XLA Ops:
  7.2 44.3 %copy-start = (bf16[256,1024]{1,0:T(8,128)(2,1)S(1)}, bf16[256,1024]{1,0:T(8,128)(2,1)}, u32[]{:S(2)}) copy-start(bf16[256,1024]{1,0:T(8,128)(2,1)} %param.3) | copy-start | bytes 1572868
  7.2 317.8 %all-reduce.4.cloned.1.call-start = ((), (), s32[]{:S(2)}) async-start(), calls=%async_computation | async-start | bytes 8388608 | tf_op jit(solution)/shard_map/psum | solution.py:79
  7.2 7.1 %collective-permute-start = (bf16[256,64]{0,1:T(8,128)(2,1)}, bf16[256,64]{0,1:T(8,128)(2,1)S(1)}, u32[]{:S(2)}, u32[]{:S(2)}) collective-permute-start(bf16[256,64]{0,1:T(8,128)(2,1)} %param.5), channel_id=1, source_target_pairs={{0,1},{1,2},{2,3},{3,4},{4,5},{5,6},{6,7},{7,8},{8,9},{9,10},{10,1... | collective-permute-start | bytes 98312 | tf_op jit(solution)/shard_map/ppermute | solution.py:66
  7.3 7.2 %collective-permute-start.1 = (bf16[256,64]{0,1:T(8,128)(2,1)}, bf16[256,64]{0,1:T(8,128)(2,1)S(1)}, u32[]{:S(2)}, u32[]{:S(2)}) collective-permute-start(bf16[256,64]{0,1:T(8,128)(2,1)} %param.5), channel_id=1, source_target_pairs={{0,15},{1,0},{2,1},{3,2},{4,3},{5,4},{6,5},{7,6},{8,7},{9,8},{10,9... | collective-permute-start | bytes 98312 | tf_op jit(solution)/shard_map/ppermute | solution.py:71
  14.3 4.6 collective-permute-start.2
  14.5 4.4 collective-permute-start.3
  18.9 4.6 collective-permute-start.4
  18.9 4.6 collective-permute-start.5
  23.4 4.6 collective-permute-start.6
  23.5 4.6 collective-permute-start.7
  28.0 4.6 collective-permute-start.8
  28.0 4.6 collective-permute-start.9
  32.6 4.6 collective-permute-start.10
  32.6 4.6 collective-permute-start.11
  37.1 4.6 collective-permute-start.12
  37.1 4.6 collective-permute-start.13
  41.7 4.6 collective-permute-start.14
  54.1 0.8 copy-start.2
  54.2 607.2 %all-reduce.6.cloned.1.call-start = ((), (), s32[]{:S(2)}) async-start(), calls=%async_computation.1 | async-start | bytes 2228224 | tf_op jit(solution)/shard_map/psum | solution.py:89
  397.6 264.5 %copy-start.1 = (bf16[256,64]{0,1:T(8,128)(2,1)S(1)}, bf16[256,64]{0,1:T(8,128)(2,1)}, u32[]{:S(2)}) copy-start(bf16[256,64]{0,1:T(8,128)(2,1)} %param.5) | copy-start | bytes 98308
Sparse Core Ops, SparseCore 0:
  54.3 270.6 all-reduce.3
  402.9 258.4 all-reduce.5
